TPU v7x, 128 devices: a whole 4x4x4 slice. The times are simulated.
128 devices in a mesh: shot: 8 (over y, core), blk: 16 (over z, x).
Axes of the slice: x: 4, y: 4, z: 4, core: 2. Of those that a mesh axis runs over, the one named last changes fastest.
Arguments:
- model_blocks: bfloat16 [16384, 2, 4, 128], P(('shot', 'blk')), may hold values from 0.19921875 to 0.3984375
- block_scales: bfloat16 [16384], P(('shot', 'blk')), may hold values from 0.75 to 1.09375
- aperture_owner: int32 [16384, 1], replicated, may hold values from 0 to 127; in each aligned block of 128 rows (0 to 127, 128 to 255, ...) at most 2 rows name the same one
- aperture_local: int32 [16384], replicated, may hold values from 0 to 127
- source_cell: int32 [8], P('shot'), may hold values from 0 to 2097151
- wavelet: float32 [8, 8], P('shot'), may hold values from -6 to 6
- receiver_cell: int32 [8, 16, 128], P('shot', 'blk'), may hold values from 0 to 131071
- observed: float32 [8, 16, 8, 128], P('shot', 'blk'), may hold values from -6 to 6
- field_now: float32 [8, 512, 32, 128], P('shot', 'blk'), may hold values from -6 to 6
- field_change: float32 [8, 512, 32, 128], P('shot', 'blk'), may hold values from -1.5 to 1.5
- adjoint_last: float32 [8, 512, 32, 128], P('shot', 'blk'), may hold values from -6 to 6
- adjoint_change: float32 [8, 512, 32, 128], P('shot', 'blk'), may hold values from -1.5 to 1.5
Outputs:
- gradient: float32 [16384, 2, 4, 128], P(('shot', 'blk'))
- field_end: float32 [8, 512, 32, 128], P('shot', 'blk')
- adjoint_first: float32 [8, 512, 32, 128], P('shot', 'blk')
Inputs may be any that keep to these rules, and one draw needn't show every extreme that they name: `aperture_owner`: among the 128 rows of one device no owner appears more than 2 times, and some owner appears exactly 2 times.
All inputs are finite; a program needn't handle non-finite values.
Results may differ from a plain program's by a relative error of at most 0.0015.
Values may be sent and summed in bfloat16 or wider, within the bound.
No kernel may reach another device: no remote copies, remote signals or barrier semaphores. Data moves between devices by JAX's collectives and lax.ppermute only.
A program may use at most 64 MiB of HBM per device.

v0:
```python
import jax
import jax.numpy as jnp
from jax import lax
from jax.sharding import PartitionSpec as P


BX = 2
BY = 4
BZ = 128
KX = 16
KY = 8
STEPS = 8
GROUP = 4


COEFFS = (-205.0 / 72.0, 8.0 / 5.0, -1.0 / 5.0, 8.0 / 315.0, -1.0 / 560.0)
GRADIENT_GAIN = 0.0625


def from_left(x):
    count = lax.axis_size("blk")
    return lax.ppermute(x, "blk", [(i, i + 1) for i in range(count - 1)])


def from_right(x):
    count = lax.axis_size("blk")
    return lax.ppermute(x, "blk", [(i + 1, i) for i in range(count - 1)])


def pack(parts):
    return jnp.concatenate([part.reshape(-1, part.shape[-1]) for part in parts], axis=0)


def unpack(buffer, likes):
    pieces, start = [], 0
    for like in likes:
        rows = like.size // like.shape[-1]
        pieces.append(buffer[start : start + rows].reshape(like.shape))
        start += rows
    return pieces


def swap(to_right, to_left):
    got_left = unpack(from_left(pack(to_right)), to_right)
    got_right = unpack(from_right(pack(to_left)), to_left)
    return got_left, got_right


def extend_all(fields):
    tails = [cells[cells.shape[0] - width :] for cells, width in fields]
    heads = [cells[:width] for cells, width in fields]
    got_left, got_right = swap(tails, heads)
    return [
        jnp.concatenate([left, cells, right], axis=0)
        for (cells, _), left, right in zip(fields, got_left, got_right)
    ]


def crop(cells, offset, want, own):
    start = offset - want
    return cells[start : start + own + 2 * want]


def lap_valid(cells):
    extent = (cells.shape[0] - 8, cells.shape[1], cells.shape[2])
    padded = jnp.pad(cells, ((0, 0), (4, 4), (4, 4)))
    centre = padded[4 : 4 + extent[0], 4 : 4 + extent[1], 4 : 4 + extent[2]]
    summed = 3.0 * COEFFS[0] * centre
    for offset in range(1, 5):
        beside_all = (
            padded[4 + offset : 4 + offset + extent[0], 4 : 4 + extent[1], 4 : 4 + extent[2]]
            + padded[4 - offset : 4 - offset + extent[0], 4 : 4 + extent[1], 4 : 4 + extent[2]]
            + padded[4 : 4 + extent[0], 4 + offset : 4 + offset + extent[1], 4 : 4 + extent[2]]
            + padded[4 : 4 + extent[0], 4 - offset : 4 - offset + extent[1], 4 : 4 + extent[2]]
            + padded[4 : 4 + extent[0], 4 : 4 + extent[1], 4 + offset : 4 + offset + extent[2]]
            + padded[4 : 4 + extent[0], 4 : 4 + extent[1], 4 - offset : 4 - offset + extent[2]]
        )
        summed = summed + COEFFS[offset] * beside_all
    return summed


def to_piece(blocks):
    return blocks.reshape(KX, KY, BX, BY, BZ).transpose(0, 2, 1, 3, 4).reshape(KX * BX, KY * BY, BZ)


def to_blocks(field_piece):
    return (
        field_piece.reshape(KX, BX, KY, BY, BZ)
        .transpose(0, 2, 1, 3, 4)
        .reshape(KX * KY, BX, BY, BZ)
    )


def one_hot_rows(index, count):
    return (index[:, None] == jnp.arange(count, dtype=index.dtype)[None, :]).astype(jnp.float32)


def exact_dot(left, right):
    return jnp.dot(left, right, precision=lax.Precision.HIGHEST, preferred_element_type=jnp.float32)


def pick_dot(one_hot, values):
    return jnp.dot(one_hot, values, precision=lax.Precision.HIGH, preferred_element_type=jnp.float32)


def local(
    model_blocks,
    block_scales,
    aperture_owner,
    aperture_local,
    source_cell,
    wavelet,
    receiver_cell,
    observed,
    field_now,
    field_change,
    adjoint_last,
    adjoint_change,
):
    devices_all = lax.axis_size(("shot", "blk"))
    my_index = lax.axis_index(("shot", "blk"))
    blk_index = lax.axis_index("blk")
    slot_count = aperture_local.shape[0] // devices_all
    cap_rows = 2
    halo = 4 * GROUP

    own, size_y, size_z = field_now.shape[1:]
    plane = size_y * size_z
    listen = receiver_cell[0, 0]
    current = field_now[0]
    before = current - field_change[0]
    listen_row = listen.astype(jnp.float32)[None, :]
    first_fields = [(current, halo), (before, halo - 4)]
    tails = [cells[own - width :] for cells, width in first_fields] + [listen_row]
    heads = [cells[:width] for cells, width in first_fields] + [listen_row]
    to_right, to_left = pack(tails), pack(heads)
    got_left = unpack(from_left(to_right), tails)
    got_right = unpack(from_right(to_left), heads)
    u_ext, b_ext = [
        jnp.concatenate([left, cells, right], axis=0)
        for (cells, _), left, right in zip(first_fields, got_left, got_right)
    ]
    adjoint_next = adjoint_last[0]
    latest = adjoint_next - adjoint_change[0]
    adjoint_fields = [(adjoint_next, halo), (latest, halo - 4)]
    adjoint_tails = [cells[own - width :] for cells, width in adjoint_fields]
    adjoint_heads = [cells[:width] for cells, width in adjoint_fields]
    adjoint_from_left = from_left(pack(adjoint_tails))
    adjoint_from_right = from_right(pack(adjoint_heads))
    listen_left = got_left[-1][0].astype(jnp.int32)
    listen_right = got_right[-1][0].astype(jnp.int32)

    owner_table = aperture_owner[:, 0].reshape(devices_all, slot_count)
    local_table = aperture_local.reshape(devices_all, slot_count)
    picked = owner_table == my_index
    count = jnp.sum(picked.astype(jnp.int32), axis=1)
    first = jnp.argmax(picked, axis=1)
    last = slot_count - 1 - jnp.argmax(picked[:, ::-1], axis=1)
    slot_iota = jnp.arange(slot_count, dtype=first.dtype)[None, :]
    lookup = jnp.stack(
        [
            jnp.sum(jnp.where(slot_iota == first[:, None], local_table, 0), axis=1),
            jnp.sum(jnp.where(slot_iota == last[:, None], local_table, 0), axis=1),
        ],
        axis=1,
    )
    filled = jnp.stack([count >= 1, count >= 2], axis=1)
    block_shape = model_blocks.shape[1:]
    block_rows = BX * BY
    owned_count = model_blocks.shape[0]
    pair_count = devices_all * cap_rows
    chooser = jnp.logical_and(
        lookup.reshape(-1)[:, None] == jnp.arange(owned_count, dtype=lookup.dtype)[None, :],
        filled.reshape(-1)[:, None],
    )
    table = jnp.concatenate(
        [
            model_blocks.reshape(owned_count, block_rows * BZ),
            jnp.broadcast_to(block_scales[:, None], (owned_count, BZ)),
        ],
        axis=1,
    )
    payload = jnp.dot(chooser.astype(table.dtype), table, preferred_element_type=jnp.float32)
    payload = payload.astype(model_blocks.dtype).reshape(devices_all, cap_rows, block_rows + 1, BZ)
    arrived = lax.all_to_all(payload, ("shot", "blk"), split_axis=0, concat_axis=0, tiled=True)

    my_owners = lax.dynamic_index_in_dim(owner_table, my_index, 0, keepdims=False)
    earlier = jnp.arange(slot_count)[None, :] < jnp.arange(slot_count)[:, None]
    my_ranks = jnp.sum(
        jnp.logical_and(my_owners[:, None] == my_owners[None, :], earlier).astype(jnp.int32), axis=1
    )
    flat_slot = my_owners * cap_rows + my_ranks
    slot_pick = flat_slot[:, None] == jnp.arange(pair_count, dtype=flat_slot.dtype)[None, :]
    rows = jnp.dot(
        slot_pick.astype(arrived.dtype), arrived.reshape(pair_count, (block_rows + 1) * BZ),
        preferred_element_type=jnp.float32,
    ).reshape(slot_count, block_rows + 1, BZ)
    values = rows[:, :block_rows].reshape((slot_count,) + block_shape)
    gain_rows = rows[:, block_rows, 0]
    scaled = values * gain_rows[:, None, None, None]
    courant = to_piece(scaled * scaled)
    (c_ext,) = extend_all([(courant, halo)])

    source_x = source_cell[0] // plane - blk_index * own
    source_rest = source_cell[0] % plane
    source_y = source_rest // size_z
    source_z = source_rest % size_z
    record = observed[0, 0]
    own_pick = one_hot_rows(listen // size_z, own * size_y)
    own_z = one_hot_rows(listen % size_z, size_z)

    snapshots = []
    misfit = []
    u_off, b_off = halo, halo - 4
    for step_index in range(STEPS):
        if step_index > 0 and step_index % GROUP == 0:
            u_ext, b_ext = extend_all([(crop(u_ext, u_off, 0, own), halo), (crop(b_ext, b_off, 0, own), halo - 4)])
            u_off, b_off = halo, halo - 4
        new_off = u_off - 4
        curved = lap_valid(u_ext)
        snapshots.append(crop(curved, new_off, 0, own))
        advanced = (
            2.0 * crop(u_ext, u_off, new_off, own)
            - crop(b_ext, b_off, new_off, own)
            + crop(c_ext, halo, new_off, own) * curved
        )
        shape_now = advanced.shape
        at_source = (
            (lax.broadcasted_iota(jnp.int32, shape_now, 0) == source_x + new_off)
            & (lax.broadcasted_iota(jnp.int32, shape_now, 1) == source_y)
            & (lax.broadcasted_iota(jnp.int32, shape_now, 2) == source_z)
        )
        advanced = advanced + jnp.where(at_source, wavelet[0, step_index], jnp.zeros((), jnp.float32))
        misfit.append(crop(advanced, new_off, 0, own).reshape(own * size_y, size_z))
        b_ext, b_off = u_ext, u_off
        u_ext, u_off = advanced, new_off
    field_end = crop(u_ext, u_off, 0, own)

    sampled = pick_dot(own_pick, jnp.concatenate(misfit, axis=1)).reshape(-1, STEPS, size_z)
    misfit_all = jnp.sum(sampled * own_z[:, None, :], axis=2).T - record
    misfit_all, adjoint_from_left, adjoint_from_right = lax.optimization_barrier(
        (misfit_all, adjoint_from_left, adjoint_from_right)
    )
    m_ext, l_ext = [
        jnp.concatenate([left, cells, right], axis=0)
        for (cells, _), left, right in zip(
            adjoint_fields,
            unpack(adjoint_from_left, adjoint_tails),
            unpack(adjoint_from_right, adjoint_heads),
        )
    ]
    (misfit_left,), (misfit_right,) = swap([misfit_all], [misfit_all])
    misfit_ext = jnp.concatenate([misfit_left, misfit_all, misfit_right], axis=1)
    cells_all = jnp.concatenate([listen_left, listen, listen_right])
    shift_all = jnp.concatenate(
        [
            jnp.full(listen.shape, -own, jnp.int32),
            jnp.zeros(listen.shape, jnp.int32),
            jnp.full(listen.shape, own, jnp.int32),
        ]
    )
    rec_x = cells_all // plane + shift_all + halo
    rec_plane = jnp.where(
        jnp.logical_and(rec_x >= 0, rec_x < own + 2 * halo), rec_x * size_y + (cells_all % plane) // size_z, -1
    )
    rec_pick = (
        jnp.arange((own + 2 * halo) * size_y, dtype=jnp.int32)[:, None] == rec_plane[None, :]
    ).astype(jnp.float32)
    rec_z = one_hot_rows(cells_all % size_z, size_z)

    injected_all = pick_dot(
        rec_pick, (rec_z[None, :, :] * misfit_ext[:, :, None]).transpose(1, 0, 2).reshape(rec_z.shape[0], -1)
    ).reshape(rec_pick.shape[0], STEPS, size_z)
    m_off, l_off = halo, halo - 4
    gradient_field = jnp.zeros_like(adjoint_next)
    for count_index, step_index in enumerate(range(STEPS - 1, -1, -1)):
        if count_index > 0 and count_index % GROUP == 0:
            m_ext, l_ext = extend_all([(crop(m_ext, m_off, 0, own), halo), (crop(l_ext, l_off, 0, own), halo - 4)])
            m_off, l_off = halo, halo - 4
        new_off = m_off - 4
        adjoint = (
            2.0 * crop(m_ext, m_off, new_off, own)
            - crop(l_ext, l_off, new_off, own)
            + lap_valid(crop(c_ext, halo, m_off, own) * m_ext)
        )
        shape_now = adjoint.shape
        first_row = (halo - new_off) * size_y
        injected = injected_all[first_row : first_row + shape_now[0] * size_y, step_index]
        adjoint = adjoint + injected.reshape(shape_now)
        gradient_field = gradient_field + crop(adjoint, new_off, 0, own) * snapshots[step_index]
        l_ext, l_off = m_ext, m_off
        m_ext, m_off = adjoint, new_off
    adjoint_first = crop(m_ext, m_off, 0, own)

    partial_blocks = to_blocks(GRADIENT_GAIN * gradient_field).reshape(slot_count, block_rows, BZ)
    parcel = exact_dot(slot_pick.T.astype(jnp.float32), partial_blocks.reshape(slot_count, block_rows * BZ))
    parcel = parcel.reshape(devices_all, cap_rows, block_rows, BZ)
    returned = lax.all_to_all(parcel, ("shot", "blk"), split_axis=0, concat_axis=0, tiled=True)
    gradient = exact_dot(chooser.T.astype(jnp.float32), returned.reshape(pair_count, -1)).reshape(model_blocks.shape)
    return (gradient, field_end[None], adjoint_first[None])


def solution(mesh):
    in_specs = (
        P(("shot", "blk"), None, None, None),
        P(("shot", "blk")),
        P(),
        P(),
        P("shot"),
        P("shot", None),
        P("shot", "blk", None),
        P("shot", "blk", None, None),
        P("shot", "blk", None, None),
        P("shot", "blk", None, None),
        P("shot", "blk", None, None),
        P("shot", "blk", None, None),
    )
    out_specs = (
        P(("shot", "blk"), None, None, None),
        P("shot", "blk", None, None),
        P("shot", "blk", None, None),
    )

    return jax.shard_map(local, mesh=mesh, in_specs=in_specs, out_specs=out_specs, check_vma=False)
```

profile of v0, /device:TPU:1, one launch (start us, length us, event | category | flops | bytes accessed | tf_op | source)
XLA Modules:
  0.0 196.0 jit_solution(18015363811095828763)
XLA Ops:
  8.6 11.9 %all-to-all-start = ((bf16[128,2,9,128]{3,1,2,0:T(2,128)(2,1)}), bf16[128,2,9,128]{3,1,2,0:T(2,128)(2,1)}, u32[]{:S(2)}, u32[]{:S(2)}) async-start(bf16[128,2,9,128]{3,1,2,0:T(2,128)(2,1)} %copy.65), calls=%async_computation | async-start | bytes 1179648 | tf_op jit(solution)/shard_map/all_to_all | solution.py:185
  22.7 4.0 %collective-permute-start = (f32[897,128]{1,0:T(8,128)}, f32[897,128]{1,0:T(8,128)}, u32[]{:S(2)}, u32[]{:S(2)}) collective-permute-start(f32[897,128]{1,0:T(8,128)} %get-tuple-element.115), channel_id=1, source_target_pairs={{0,1},{1,2},{2,3},{3,4},{4,5},{5,6},{6,7},{7,8},{8,9},{9,10},{10,1... | collective-permute-start | bytes 1377800 | tf_op jit(solution)/shard_map/ppermute | solution.py:22
  30.2 4.8 %collective-permute-start.6 = (f32[896,128]{1,0:T(8,128)}, f32[896,128]{1,0:T(8,128)}, u32[]{:S(2)}, u32[]{:S(2)}) collective-permute-start(f32[896,128]{1,0:T(8,128)} %pad_maximum_fusion.9), channel_id=1, source_target_pairs={{0,1},{1,2},{2,3},{3,4},{4,5},{5,6},{6,7},{7,8},{8,9},{9,10},{10,1... | collective-permute-start | bytes 1376264 | tf_op jit(solution)/shard_map/ppermute | solution.py:22
  48.4 3.9 %collective-permute-start.2 = (f32[512,128]{1,0:T(8,128)S(1)}, f32[512,128]{1,0:T(8,128)S(1)}, u32[]{:S(2)}, u32[]{:S(2)}) collective-permute-start(f32[512,128]{1,0:T(8,128)S(1)} %bitcast.250), channel_id=1, source_target_pairs={{0,1},{1,2},{2,3},{3,4},{4,5},{5,6},{6,7},{7,8},{8,9},{9,10},{10,1... | collective-permute-start | bytes 786440 | tf_op jit(solution)/shard_map/ppermute | solution.py:22
  56.4 3.8 %collective-permute-done.3 = f32[512,128]{1,0:T(8,128)S(1)} collective-permute-done((f32[512,128]{1,0:T(8,128)S(1)}, f32[512,128]{1,0:T(8,128)S(1)}, u32[]{:S(2)}, u32[]{:S(2)}) %collective-permute-start.3) | collective-permute-done | bytes 262176 | tf_op jit(solution)/shard_map/ppermute | solution.py:27
  60.4 4.1 %fusion.109 = (f32[56,32,128]{2,1,0:T(8,128)S(1)}, f32[56,32,128]{2,1,0:T(8,128)}) fusion(f32[12,32,128]{2,1,0:T(8,128)S(1)} %bitcast.245, f32[32,32,128]{2,1,0:T(8,128)S(1)} %bitcast_subtract_fusion.1, f32[12,32,128]{2,1,0:T(8,128)S(1)} %bitcast.244, f32[64,32,128]{2,1,0:T(8,128)S(1)} %pad_maximum_fusion, f32[64,32,128]{2,1,0:T(8,128)S(1)} %pad_maximum_fusion.1, ...), kind=kLoop, calls=%fused_computation.394 | loop fusion | flops 8945664 | bytes 12977668 | tf_op jit(solution)/shard_map/add | solution.py:233
  64.5 3.3 %fusion.215 = (f32[48,32,128]{2,1,0:T(8,128)S(1)}, f32[48,32,128]{2,1,0:T(8,128)}) fusion(f32[64,32,128]{2,1,0:T(8,128)S(1)} %pad_maximum_fusion, f32[56,32,128]{2,1,0:T(8,128)S(1)} %get-tuple-element.61, f32[64,32,128]{2,1,0:T(8,128)S(1)} %pad_maximum_fusion.1, f32[]{:T(128)} %bitcast.36, pred[128]{0:T(512)(128)(4,1)S(1)} %iota_compare_fusion.13, ...), kind=kLoop, calls=%fused_computation.526 | loop fusion | flops 7274496 | bytes 11142660 | tf_op jit(solution)/shard_map/add | solution.py:233
  67.8 3.0 %fusion.321 = (f32[40,32,128]{2,1,0:T(8,128)S(1)}, f32[40,32,128]{2,1,0:T(8,128)}) fusion(f32[56,32,128]{2,1,0:T(8,128)S(1)} %get-tuple-element.61, f32[48,32,128]{2,1,0:T(8,128)S(1)} %get-tuple-element.59, f32[64,32,128]{2,1,0:T(8,128)S(1)} %pad_maximum_fusion.1, f32[]{:T(128)} %bitcast.38, pred[128]{0:T(512)(128)(4,1)S(1)} %iota_compare_fusion.13, ...), kind=kLoop, calls=%fused_computation.661 | loop fusion | flops 6062080 | bytes 9307652 | tf_op jit(solution)/shard_map/add | solution.py:233
  70.9 2.6 %select_add_fusion.1 = (f32[32,32,128]{2,1,0:T(8,128)S(1)}, f32[32,32,128]{2,1,0:T(8,128)}, f32[32,32,128]{2,1,0:T(8,128)S(1)}, f32[32,32,128]{2,1,0:T(8,128)S(1)}) fusion(f32[32,32,128]{2,1,0:T(8,128)S(1)} %bitcast.175, f32[]{:T(128)} %bitcast.41, pred[128]{0:T(512)(128)(4,1)S(1)} %iota_compare_fusion.13, pred[32]{0:T(512)(128)(4,1)S(1)} %iota_compare_fusion.14, ...), kind=kLoop, calls=%fused_computation.808 | loop fusion | flops 4849664 | bytes 8521220 | tf_op jit(solution)/shard_map/add | solution.py:233
  73.6 3.5 %collective-permute-start.4 = (f32[896,128]{1,0:T(8,128)S(1)}, f32[896,128]{1,0:T(8,128)S(1)}, u32[]{:S(2)}, u32[]{:S(2)}) collective-permute-start(f32[896,128]{1,0:T(8,128)S(1)} %pad_maximum_fusion.7), channel_id=1, source_target_pairs={{0,1},{1,2},{2,3},{3,4},{4,5},{5,6},{6,7},{7,8},{8,9},{9,10},{10,1... | collective-permute-start | bytes 1376264 | tf_op jit(solution)/shard_map/ppermute | solution.py:22
  77.1 1.5 collective-permute-start.5
  78.9 5.6 %collective-permute-done.4 = f32[896,128]{1,0:T(8,128)S(1)} collective-permute-done((f32[896,128]{1,0:T(8,128)S(1)}, f32[896,128]{1,0:T(8,128)S(1)}, u32[]{:S(2)}, u32[]{:S(2)}) %collective-permute-start.4) | collective-permute-done | bytes 458784 | tf_op jit(solution)/shard_map/ppermute | solution.py:22
  84.5 6.0 %collective-permute-done.5 = f32[896,128]{1,0:T(8,128)S(1)} collective-permute-done((f32[896,128]{1,0:T(8,128)S(1)}, f32[896,128]{1,0:T(8,128)S(1)}, u32[]{:S(2)}, u32[]{:S(2)}) %collective-permute-start.5) | collective-permute-done | bytes 458784 | tf_op jit(solution)/shard_map/ppermute | solution.py:27
  90.7 4.1 %fusion.111 = (f32[56,32,128]{2,1,0:T(8,128)S(1)}, f32[56,32,128]{2,1,0:T(8,128)}) fusion(f32[12,32,128]{2,1,0:T(8,128)S(1)} %bitcast.247, f32[32,32,128]{2,1,0:T(8,128)S(1)} %get-tuple-element.79, f32[12,32,128]{2,1,0:T(8,128)S(1)} %bitcast.246, f32[64,32,128]{2,1,0:T(8,128)S(1)} %pad_maximum_fusion.2, f32[64,32,128]{2,1,0:T(8,128)S(1)} %pad_maximum_fusion.1, ...), kind=kLoop, calls=%fused_computation.397 | loop fusion | flops 8945664 | bytes 12977668 | tf_op jit(solution)/shard_map/add | solution.py:233
  94.8 3.3 %fusion.213 = (f32[48,32,128]{2,1,0:T(8,128)S(1)}, f32[48,32,128]{2,1,0:T(8,128)}) fusion(f32[64,32,128]{2,1,0:T(8,128)S(1)} %pad_maximum_fusion.2, f32[56,32,128]{2,1,0:T(8,128)S(1)} %get-tuple-element.53, f32[64,32,128]{2,1,0:T(8,128)S(1)} %pad_maximum_fusion.1, f32[]{:T(128)} %bitcast.53, pred[128]{0:T(512)(128)(4,1)S(1)} %iota_compare_fusion.13, ...), kind=kLoop, calls=%fused_computation.519 | loop fusion | flops 7274496 | bytes 11142660 | tf_op jit(solution)/shard_map/add | solution.py:233
  98.2 2.9 %fusion.319 = (f32[40,32,128]{2,1,0:T(8,128)S(1)}, f32[40,32,128]{2,1,0:T(8,128)}) fusion(f32[56,32,128]{2,1,0:T(8,128)S(1)} %get-tuple-element.53, f32[48,32,128]{2,1,0:T(8,128)S(1)} %get-tuple-element.51, f32[64,32,128]{2,1,0:T(8,128)S(1)} %pad_maximum_fusion.1, f32[]{:T(128)} %bitcast.55, pred[128]{0:T(512)(128)(4,1)S(1)} %iota_compare_fusion.13, ...), kind=kLoop, calls=%fused_computation.654 | loop fusion | flops 6062080 | bytes 9307652 | tf_op jit(solution)/shard_map/add | solution.py:233
  101.1 2.6 %select_add_fusion = (f32[32,32,128]{2,1,0:T(8,128)S(1)}, f32[32,32,128]{2,1,0:T(8,128)}, f32[32,32,128]{2,1,0:T(8,128)S(1)}, f32[32,32,128]{2,1,0:T(8,128)S(1)}) fusion(f32[32,32,128]{2,1,0:T(8,128)S(1)} %bitcast.176, f32[]{:T(128)} %bitcast.57, pred[128]{0:T(512)(128)(4,1)S(1)} %iota_compare_fusion.13, pred[32]{0:T(512)(128)(4,1)S(1)} %iota_compare_fusion.14, ...), kind=kLoop, calls=%fused_computation.807 | loop fusion | flops 4849664 | bytes 8521220 | tf_op jit(solution)/shard_map/add | solution.py:233
  105.4 4.9 %collective-permute-start.8 = (f32[8,128]{0,1:T(8,128)S(1)}, f32[8,128]{0,1:T(8,128)S(1)}, u32[]{:S(2)}, u32[]{:S(2)}) collective-permute-start(f32[8,128]{0,1:T(8,128)S(1)} %bitcast_subtract_fusion.2), channel_id=1, source_target_pairs={{0,1},{1,2},{2,3},{3,4},{4,5},{5,6},{6,7},{7,8},{8,9},{9,10},{10,1... | collective-permute-start | bytes 12296 | tf_op jit(solution)/shard_map/ppermute | solution.py:22
  110.3 1.5 collective-permute-start.9
  117.0 4.8 %fusion.1 = f32[2048,8,128]{2,0,1:T(8,128)S(1)} fusion(s32[384]{0:T(512)S(1)} %get-tuple-element.102, f32[384,8]{0,1:T(8,128)S(1)} %maximum_bitcast_fusion, f32[384,128]{0,1:T(8,128)S(1)} %fusion.435), kind=kOutput, calls=%fused_computation.258 | convolution fusion | flops 4833017856 | bytes 8599040 | tf_op jit(solution)/shard_map/dot_general | solution.py:103
  123.3 2.6 %slice_multiply_fusion.9 = (f32[56,32,128]{2,1,0:T(8,128)S(1)}, f32[56,32,128]{2,1,0:T(8,128)S(1)}) fusion(f32[64,32,128]{2,1,0:T(8,128)S(1)} %pad_maximum_fusion.1, f32[56,32,128]{2,1,0:T(8,128)S(1)} %bitcast.190, f32[64,32,128]{2,1,0:T(8,128)S(1)} %get-tuple-element.76, f32[12,32,128]{2,1,0:T(8,128)S(1)} %bitcast.233, f32[32,32,128]{2,1,0:T(8,128)S(1)} %copy-done.4, ...), kind=kLoop, calls=%fused_computation.531 | loop fusion | flops 8257536 | bytes 14811136 | tf_op jit(solution)/shard_map/mul | solution.py:284
  125.9 1.9 slice_multiply_fusion.15
  127.8 1.6 slice_multiply_fusion.17
  130.7 4.0 %collective-permute-start.10 = (f32[896,128]{1,0:T(8,128)S(1)}, f32[896,128]{1,0:T(8,128)S(1)}, u32[]{:S(2)}, u32[]{:S(2)}) collective-permute-start(f32[896,128]{1,0:T(8,128)S(1)} %pad_maximum_fusion.11), channel_id=1, source_target_pairs={{0,1},{1,2},{2,3},{3,4},{4,5},{5,6},{6,7},{7,8},{8,9},{9,10},{10,1... | collective-permute-start | bytes 1376264 | tf_op jit(solution)/shard_map/ppermute | solution.py:22
  134.8 1.6 collective-permute-start.11
  136.3 4.2 %collective-permute-done.10 = f32[896,128]{1,0:T(8,128)S(1)} collective-permute-done((f32[896,128]{1,0:T(8,128)S(1)}, f32[896,128]{1,0:T(8,128)S(1)}, u32[]{:S(2)}, u32[]{:S(2)}) %collective-permute-start.10) | collective-permute-done | bytes 458784 | tf_op jit(solution)/shard_map/ppermute | solution.py:22
  140.5 5.1 %collective-permute-done.11 = f32[896,128]{1,0:T(8,128)S(1)} collective-permute-done((f32[896,128]{1,0:T(8,128)S(1)}, f32[896,128]{1,0:T(8,128)S(1)}, u32[]{:S(2)}, u32[]{:S(2)}) %collective-permute-start.11) | collective-permute-done | bytes 458784 | tf_op jit(solution)/shard_map/ppermute | solution.py:27
  145.9 2.6 %slice_multiply_fusion.8 = (f32[56,32,128]{2,1,0:T(8,128)S(1)}, f32[56,32,128]{2,1,0:T(8,128)S(1)}) fusion(f32[64,32,128]{2,1,0:T(8,128)S(1)} %pad_maximum_fusion.1, f32[56,32,128]{2,1,0:T(8,128)S(1)} %bitcast.189, f32[64,32,128]{2,1,0:T(8,128)S(1)} %get-tuple-element.74, f32[12,32,128]{2,1,0:T(8,128)S(1)} %bitcast.235, ...), kind=kLoop, calls=%fused_computation.530 | loop fusion | flops 8257536 | bytes 14811136 | tf_op jit(solution)/shard_map/mul | solution.py:284
  148.5 1.9 slice_multiply_fusion.14
  150.5 1.6 slice_multiply_fusion.16
  153.0 2.7 %fusion.423 = (f32[32,32,128]{2,1,0:T(8,128)S(1)}, f32[32,32,128]{2,1,0:T(8,128)}) fusion(f32[56,32,128]{2,1,0:T(8,128)S(1)} %copy-done.9, f32[48,32,128]{2,1,0:T(8,128)S(1)} %copy-done.11, f32[40,32,128]{2,1,0:T(8,128)S(1)} %copy-done.13, f32[32,32,128]{2,1,0:T(8,128)S(1)} %copy-done.15, f32[56,32,128]{2,1,0:T(8,128)S(1)} %get-tuple-element.40, ...), kind=kLoop, calls=%fused_computation.770 | loop fusion | flops 6422528 | bytes 14811136 | tf_op jit(solution)/shard_map/mul | solution.py:295
  157.2 36.4 %all_to_all.10 = f32[128,2,8,128]{3,2,1,0:T(8,128)S(1)} all-to-all(f32[128,2,8,128]{3,2,1,0:T(8,128)S(1)} %copy.75), channel_id=1, replica_groups=mesh['shot'=8,'blk'=16] {'shot','blk'}, dimensions={0} | all-to-all | bytes 2097152 | tf_op jit(solution)/shard_map/all_to_all | solution.py:298
  (171 shorter events, 45.3 us)
Async XLA Ops:
  0.6 19.8 %copy-start.1 = (f32[1,32,32,128]{3,2,1,0:T(8,128)S(1)}, f32[1,32,32,128]{3,2,1,0:T(8,128)}, u32[]{:S(2)}) copy-start(f32[1,32,32,128]{3,2,1,0:T(8,128)} %param.20) | copy-start | bytes 1572868
  6.5 15.2 %copy-start.21 = (s32[1,1,128]{2,1,0:T(1,128)S(1)}, s32[1,1,128]{2,1,0:T(1,128)}, u32[]{:S(2)}) copy-start(s32[1,1,128]{2,1,0:T(1,128)} %param.18) | copy-start | bytes 1540
  7.2 20.8 %copy-start.2 = (f32[1,32,32,128]{3,2,1,0:T(8,128)S(1)}, f32[1,32,32,128]{3,2,1,0:T(8,128)}, u32[]{:S(2)}) copy-start(f32[1,32,32,128]{3,2,1,0:T(8,128)} %param.22) | copy-start | bytes 1572868
  8.6 35.2 %all-to-all-start = ((bf16[128,2,9,128]{3,1,2,0:T(2,128)(2,1)}), bf16[128,2,9,128]{3,1,2,0:T(2,128)(2,1)}, u32[]{:S(2)}, u32[]{:S(2)}) async-start(bf16[128,2,9,128]{3,1,2,0:T(2,128)(2,1)} %copy.65), calls=%async_computation | async-start | bytes 1179648 | tf_op jit(solution)/shard_map/all_to_all | solution.py:185
  21.6 17.8 %copy-start.18 = (f32[1,8]{1,0:T(1,128)S(1)}, f32[1,8]{1,0:T(1,128)}, u32[]{:S(2)}) copy-start(f32[1,8]{1,0:T(1,128)} %param.17) | copy-start | bytes 100
  21.7 18.5 %copy-start.19 = (f32[1,1,8,128]{3,2,1,0:T(8,128)S(1)}, f32[1,1,8,128]{3,2,1,0:T(8,128)}, u32[]{:S(2)}) copy-start(f32[1,1,8,128]{3,2,1,0:T(8,128)} %param.19) | copy-start | bytes 12292
  21.7 22.0 %copy-start.20 = (s32[384]{0:T(512)S(1)}, s32[384]{0:T(512)}, u32[]{:S(2)}) copy-start(s32[384]{0:T(512)} %constant.170.clone.1) | copy-start | bytes 4612
  22.7 19.4 %collective-permute-start = (f32[897,128]{1,0:T(8,128)}, f32[897,128]{1,0:T(8,128)}, u32[]{:S(2)}, u32[]{:S(2)}) collective-permute-start(f32[897,128]{1,0:T(8,128)} %get-tuple-element.115), channel_id=1, source_target_pairs={{0,1},{1,2},{2,3},{3,4},{4,5},{5,6},{6,7},{7,8},{8,9},{9,10},{10,1... | collective-permute-start | bytes 1377800 | tf_op jit(solution)/shard_map/ppermute | solution.py:22
  26.7 13.7 %collective-permute-start.1 = (f32[897,128]{1,0:T(8,128)}, f32[897,128]{1,0:T(8,128)}, u32[]{:S(2)}, u32[]{:S(2)}) collective-permute-start(f32[897,128]{1,0:T(8,128)} %get-tuple-element.116), channel_id=1, source_target_pairs={{1,0},{2,1},{3,2},{4,3},{5,4},{6,5},{7,6},{8,7},{9,8},{10,9},{11,1... | collective-permute-start | bytes 1377800 | tf_op jit(solution)/shard_map/ppermute | solution.py:27
  29.2 14.6 %copy-start.3 = (f32[32,32,128]{2,1,0:T(8,128)}, f32[32,32,128]{2,1,0:T(8,128)S(1)}, u32[]{:S(2)}) copy-start(f32[32,32,128]{2,1,0:T(8,128)S(1)} %bitcast_subtract_fusion) | copy-start | bytes 1572868
  30.2 75.2 %collective-permute-start.6 = (f32[896,128]{1,0:T(8,128)}, f32[896,128]{1,0:T(8,128)}, u32[]{:S(2)}, u32[]{:S(2)}) collective-permute-start(f32[896,128]{1,0:T(8,128)} %pad_maximum_fusion.9), channel_id=1, source_target_pairs={{0,1},{1,2},{2,3},{3,4},{4,5},{5,6},{6,7},{7,8},{8,9},{9,10},{10,1... | collective-permute-start | bytes 1376264 | tf_op jit(solution)/shard_map/ppermute | solution.py:22
  35.8 69.6 %collective-permute-start.7 = (f32[896,128]{1,0:T(8,128)}, f32[896,128]{1,0:T(8,128)}, u32[]{:S(2)}, u32[]{:S(2)}) collective-permute-start(f32[896,128]{1,0:T(8,128)} %pad_maximum_fusion.10), channel_id=1, source_target_pairs={{1,0},{2,1},{3,2},{4,3},{5,4},{6,5},{7,6},{8,7},{9,8},{10,9},{11,1... | collective-permute-start | bytes 1376264 | tf_op jit(solution)/shard_map/ppermute | solution.py:27
  48.4 8.1 %collective-permute-start.2 = (f32[512,128]{1,0:T(8,128)S(1)}, f32[512,128]{1,0:T(8,128)S(1)}, u32[]{:S(2)}, u32[]{:S(2)}) collective-permute-start(f32[512,128]{1,0:T(8,128)S(1)} %bitcast.250), channel_id=1, source_target_pairs={{0,1},{1,2},{2,3},{3,4},{4,5},{5,6},{6,7},{7,8},{8,9},{9,10},{10,1... | collective-permute-start | bytes 786440 | tf_op jit(solution)/shard_map/ppermute | solution.py:22
  52.3 8.0 %collective-permute-start.3 = (f32[512,128]{1,0:T(8,128)S(1)}, f32[512,128]{1,0:T(8,128)S(1)}, u32[]{:S(2)}, u32[]{:S(2)}) collective-permute-start(f32[512,128]{1,0:T(8,128)S(1)} %bitcast.249), channel_id=1, source_target_pairs={{1,0},{2,1},{3,2},{4,3},{5,4},{6,5},{7,6},{8,7},{9,8},{10,9},{11,1... | collective-permute-start | bytes 786440 | tf_op jit(solution)/shard_map/ppermute | solution.py:27
  56.4 57.3 %copy-start.5 = (f32[512,128]{1,0:T(8,128)}, f32[512,128]{1,0:T(8,128)S(1)}, u32[]{:S(2)}) copy-start(f32[512,128]{1,0:T(8,128)S(1)} %collective-permute-done.2) | copy-start | bytes 786436
  60.3 53.5 %copy-start.7 = (f32[512,128]{1,0:T(8,128)}, f32[512,128]{1,0:T(8,128)S(1)}, u32[]{:S(2)}) copy-start(f32[512,128]{1,0:T(8,128)S(1)} %collective-permute-done.3) | copy-start | bytes 786436
  73.6 10.9 %collective-permute-start.4 = (f32[896,128]{1,0:T(8,128)S(1)}, f32[896,128]{1,0:T(8,128)S(1)}, u32[]{:S(2)}, u32[]{:S(2)}) collective-permute-start(f32[896,128]{1,0:T(8,128)S(1)} %pad_maximum_fusion.7), channel_id=1, source_target_pairs={{0,1},{1,2},{2,3},{3,4},{4,5},{5,6},{6,7},{7,8},{8,9},{9,10},{10,1... | collective-permute-start | bytes 1376264 | tf_op jit(solution)/shard_map/ppermute | solution.py:22
  77.1 13.5 %collective-permute-start.5 = (f32[896,128]{1,0:T(8,128)S(1)}, f32[896,128]{1,0:T(8,128)S(1)}, u32[]{:S(2)}, u32[]{:S(2)}) collective-permute-start(f32[896,128]{1,0:T(8,128)S(1)} %pad_maximum_fusion.8), channel_id=1, source_target_pairs={{1,0},{2,1},{3,2},{4,3},{5,4},{6,5},{7,6},{8,7},{9,8},{10,9},{11,1... | collective-permute-start | bytes 1376264 | tf_op jit(solution)/shard_map/ppermute | solution.py:27
  105.4 11.6 %collective-permute-start.8 = (f32[8,128]{0,1:T(8,128)S(1)}, f32[8,128]{0,1:T(8,128)S(1)}, u32[]{:S(2)}, u32[]{:S(2)}) collective-permute-start(f32[8,128]{0,1:T(8,128)S(1)} %bitcast_subtract_fusion.2), channel_id=1, source_target_pairs={{0,1},{1,2},{2,3},{3,4},{4,5},{5,6},{6,7},{7,8},{8,9},{9,10},{10,1... | collective-permute-start | bytes 12296 | tf_op jit(solution)/shard_map/ppermute | solution.py:22
  110.3 6.7 %collective-permute-start.9 = (f32[8,128]{0,1:T(8,128)S(1)}, f32[8,128]{0,1:T(8,128)S(1)}, u32[]{:S(2)}, u32[]{:S(2)}) collective-permute-start(f32[8,128]{0,1:T(8,128)S(1)} %bitcast_subtract_fusion.2), channel_id=1, source_target_pairs={{1,0},{2,1},{3,2},{4,3},{5,4},{6,5},{7,6},{8,7},{9,8},{10,9},{11,1... | collective-permute-start | bytes 12296 | tf_op jit(solution)/shard_map/ppermute | solution.py:27
  129.4 16.2 %copy-start.6 = (f32[512,128]{1,0:T(8,128)S(1)}, f32[512,128]{1,0:T(8,128)}, u32[]{:S(2)}) copy-start(f32[512,128]{1,0:T(8,128)} %copy-done.5) | copy-start | bytes 786436
  129.4 16.2 %copy-start.8 = (f32[512,128]{1,0:T(8,128)S(1)}, f32[512,128]{1,0:T(8,128)}, u32[]{:S(2)}) copy-start(f32[512,128]{1,0:T(8,128)} %copy-done.7) | copy-start | bytes 786436
  130.7 9.8 %collective-permute-start.10 = (f32[896,128]{1,0:T(8,128)S(1)}, f32[896,128]{1,0:T(8,128)S(1)}, u32[]{:S(2)}, u32[]{:S(2)}) collective-permute-start(f32[896,128]{1,0:T(8,128)S(1)} %pad_maximum_fusion.11), channel_id=1, source_target_pairs={{0,1},{1,2},{2,3},{3,4},{4,5},{5,6},{6,7},{7,8},{8,9},{9,10},{10,1... | collective-permute-start | bytes 1376264 | tf_op jit(solution)/shard_map/ppermute | solution.py:22
  134.8 10.8 %collective-permute-start.11 = (f32[896,128]{1,0:T(8,128)S(1)}, f32[896,128]{1,0:T(8,128)S(1)}, u32[]{:S(2)}, u32[]{:S(2)}) collective-permute-start(f32[896,128]{1,0:T(8,128)S(1)} %pad_maximum_fusion.12), channel_id=1, source_target_pairs={{1,0},{2,1},{3,2},{4,3},{5,4},{6,5},{7,6},{8,7},{9,8},{10,9},{11,1... | collective-permute-start | bytes 1376264 | tf_op jit(solution)/shard_map/ppermute | solution.py:27
  150.4 1.7 copy-start.9
  150.4 1.7 copy-start.10
  150.4 1.7 copy-start.11
  150.4 1.9 copy-start.12
  150.4 2.1 %copy-start.13 = (f32[40,32,128]{2,1,0:T(8,128)S(1)}, f32[40,32,128]{2,1,0:T(8,128)}, u32[]{:S(2)}) copy-start(f32[40,32,128]{2,1,0:T(8,128)} %get-tuple-element.58) | copy-start | bytes 1966084
  150.4 2.3 %copy-start.14 = (f32[40,32,128]{2,1,0:T(8,128)S(1)}, f32[40,32,128]{2,1,0:T(8,128)}, u32[]{:S(2)}) copy-start(f32[40,32,128]{2,1,0:T(8,128)} %get-tuple-element.50) | copy-start | bytes 1966084
  150.5 2.4 %copy-start.15 = (f32[32,32,128]{2,1,0:T(8,128)S(1)}, f32[32,32,128]{2,1,0:T(8,128)}, u32[]{:S(2)}) copy-start(f32[32,32,128]{2,1,0:T(8,128)} %get-tuple-element.56) | copy-start | bytes 1572868
  150.5 2.6 %copy-start.16 = (f32[32,32,128]{2,1,0:T(8,128)S(1)}, f32[32,32,128]{2,1,0:T(8,128)}, u32[]{:S(2)}) copy-start(f32[32,32,128]{2,1,0:T(8,128)} %get-tuple-element.48) | copy-start | bytes 1572868
  (3 other events, 3.9 us)
where the time goes:
time: 197 us; the launch traced here: 196 us
  other arithmetic  55.4 us (28%)
  starting transfers between devices  45.4 us (23%)
  blocking collectives  36.4 us (18%)
  waiting for transfers between devices  25.3 us (13%)
  local copies, waits for them, and re-layouts  23.3 us (12%)
  matrix products  7.83 us (4%)
  between operations  2.37 us (1%)
    all_to_all x1, blocking collectives, local(): lax.all_to_all(parcel, ('shot', 'blk'), split_axis=0, concat_axis=0, tile...  36.4 us
    add x8, other arithmetic, local(): advanced + jnp.where(at_source, wavelet[0, step_index], jnp.zeros((), jnp...  26 us
    ppermute x6, starting transfers between devices, from_left(): return lax.ppermute(x, 'blk', [(i, i + 1) for i in range(count - 1)])  25.1 us
    ppermute x6, waiting for transfers between devices, from_right(): return lax.ppermute(x, 'blk', [(i + 1, i) for i in range(count - 1)])  15 us
    mul x6, other arithmetic, local(): crop(c_ext, halo, m_off, own) * m_ext  12.1 us
    all_to_all x1, starting transfers between devices, local(): lax.all_to_all(payload, ('shot', 'blk'), split_axis=0, concat_axis=0, til...  11.9 us
    ppermute x6, waiting for transfers between devices, from_left(): return lax.ppermute(x, 'blk', [(i, i + 1) for i in range(count - 1)])  10.3 us
    ppermute x6, starting transfers between devices, from_right(): return lax.ppermute(x, 'blk', [(i + 1, i) for i in range(count - 1)])  8.39 us
  transfers between devices with their start and end apart: 13, of which 7 were waited for; matrix products, arithmetic and copies ran while one was open for 26% of the time, Pallas kernels for 0%

commit v1 on v0

--- a/solution.py
+++ b/solution.py
@@ -268,9 +268,11 @@
     ).astype(jnp.float32)
     rec_z = one_hot_rows(cells_all % size_z, size_z)
 
-    injected_all = pick_dot(
-        rec_pick, (rec_z[None, :, :] * misfit_ext[:, :, None]).transpose(1, 0, 2).reshape(rec_z.shape[0], -1)
-    ).reshape(rec_pick.shape[0], STEPS, size_z)
+    def injections(steps):
+        values = (rec_z[None, :, :] * misfit_ext[steps, :, None]).transpose(1, 0, 2).reshape(rec_z.shape[0], -1)
+        return pick_dot(rec_pick, values).reshape(rec_pick.shape[0], len(steps), size_z)
+
+    injected_groups = {}
     m_off, l_off = halo, halo - 4
     gradient_field = jnp.zeros_like(adjoint_next)
     for count_index, step_index in enumerate(range(STEPS - 1, -1, -1)):
@@ -285,7 +287,11 @@
         )
         shape_now = adjoint.shape
         first_row = (halo - new_off) * size_y
-        injected = injected_all[first_row : first_row + shape_now[0] * size_y, step_index]
+        group_index = count_index // GROUP
+        if group_index not in injected_groups:
+            group_steps = list(range(STEPS - 1 - group_index * GROUP, STEPS - 1 - (group_index + 1) * GROUP, -1))
+            injected_groups[group_index] = injections(group_steps)
+        injected = injected_groups[group_index][first_row : first_row + shape_now[0] * size_y, count_index % GROUP]
         adjoint = adjoint + injected.reshape(shape_now)
         gradient_field = gradient_field + crop(adjoint, new_off, 0, own) * snapshots[step_index]
         l_ext, l_off = m_ext, m_off

time: 197 us -> 203 us (1.030)
  waiting for transfers between devices: 25.3 us -> 19.5 us
  local copies, waits for them, and re-layouts: 23.3 us -> 29 us
  other arithmetic: 55.4 us -> 60.2 us
    slice x16, local copies, waits for them, and re-layouts: 7.79 us -> 12.9 us  [unpack(): pieces.append(buffer[start:start + rows].reshape(like.shape))]
    ppermute x6, waiting for transfers between devices: 10.3 us -> 6.33 us  [from_left(): return lax.ppermute(x, 'blk', [(i, i + 1) for i in range(count - 1)])]
    unnamed x56 -> x97, local copies, waits for them, and re-layouts: 5.03 us -> 4.52 us
    dot_general x2 -> x3, matrix products: 5.8 us -> 5.92 us  [pick_dot(): jnp.dot(one_hot, values, precision=lax.Precision.HIGH, preferred_element_...]
  transfers between devices with their start and end apart: 13 -> 13, of which waited for: 7 -> 5; matrix products, arithmetic and copies ran while one was open for 26% -> 30% of each run, Pallas kernels for 0% -> 0%
where the time goes in v1:
time: 203 us; the launch traced here: 202 us
  other arithmetic  60.2 us (30%)
  starting transfers between devices  45.9 us (23%)
  blocking collectives  36.9 us (18%)
  local copies, waits for them, and re-layouts  29 us (14%)
  waiting for transfers between devices  19.5 us (10%)
  matrix products  7.95 us (4%)
  between operations  2.6 us (1%)
    all_to_all x1, blocking collectives, local(): lax.all_to_all(parcel, ('shot', 'blk'), split_axis=0, concat_axis=0, tile...  36.9 us
    add x8, other arithmetic, local(): advanced + jnp.where(at_source, wavelet[0, step_index], jnp.zeros((), jnp...  26.1 us
    ppermute x6, starting transfers between devices, from_left(): return lax.ppermute(x, 'blk', [(i, i + 1) for i in range(count - 1)])  25.9 us
    ppermute x6, waiting for transfers between devices, from_right(): return lax.ppermute(x, 'blk', [(i + 1, i) for i in range(count - 1)])  13.2 us
    slice x16, local copies, waits for them, and re-layouts, unpack(): pieces.append(buffer[start:start + rows].reshape(like.shape))  12.9 us
    mul x6, other arithmetic, local(): crop(c_ext, halo, m_off, own) * m_ext  12.2 us
    all_to_all x1, starting transfers between devices, local(): lax.all_to_all(payload, ('shot', 'blk'), split_axis=0, concat_axis=0, til...  11.9 us
    ppermute x6, starting transfers between devices, from_right(): return lax.ppermute(x, 'blk', [(i + 1, i) for i in range(count - 1)])  8.12 us
  transfers between devices with their start and end apart: 13, of which 5 were waited for; matrix products, arithmetic and copies ran while one was open for 30% of the time, Pallas kernels for 0%

profile of v1, /device:TPU:1, one launch (start us, length us, event | category | flops | bytes accessed | tf_op | source)
XLA Modules:
  0.0 202.1 jit_solution(11701624803571910997)
XLA Ops:
  8.6 11.9 %all-to-all-start = ((bf16[128,2,9,128]{3,1,2,0:T(2,128)(2,1)}), bf16[128,2,9,128]{3,1,2,0:T(2,128)(2,1)}, u32[]{:S(2)}, u32[]{:S(2)}) async-start(bf16[128,2,9,128]{3,1,2,0:T(2,128)(2,1)} %copy.51), calls=%async_computation | async-start | bytes 1179648 | tf_op jit(solution)/shard_map/all_to_all | solution.py:185
  22.7 4.0 %collective-permute-start = (f32[897,128]{1,0:T(8,128)}, f32[897,128]{1,0:T(8,128)}, u32[]{:S(2)}, u32[]{:S(2)}) collective-permute-start(f32[897,128]{1,0:T(8,128)} %get-tuple-element.104), channel_id=1, source_target_pairs={{0,1},{1,2},{2,3},{3,4},{4,5},{5,6},{6,7},{7,8},{8,9},{9,10},{10,1... | collective-permute-start | bytes 1377800 | tf_op jit(solution)/shard_map/ppermute | solution.py:22
  30.2 4.7 %collective-permute-start.6 = (f32[896,128]{1,0:T(8,128)}, f32[896,128]{1,0:T(8,128)}, u32[]{:S(2)}, u32[]{:S(2)}) collective-permute-start(f32[896,128]{1,0:T(8,128)} %pad_maximum_fusion.9), channel_id=1, source_target_pairs={{0,1},{1,2},{2,3},{3,4},{4,5},{5,6},{6,7},{7,8},{8,9},{9,10},{10,1... | collective-permute-start | bytes 1376264 | tf_op jit(solution)/shard_map/ppermute | solution.py:22
  48.9 4.0 %collective-permute-start.2 = (f32[512,128]{1,0:T(8,128)S(1)}, f32[512,128]{1,0:T(8,128)S(1)}, u32[]{:S(2)}, u32[]{:S(2)}) collective-permute-start(f32[512,128]{1,0:T(8,128)S(1)} %bitcast.258), channel_id=1, source_target_pairs={{0,1},{1,2},{2,3},{3,4},{4,5},{5,6},{6,7},{7,8},{8,9},{9,10},{10,1... | collective-permute-start | bytes 786440 | tf_op jit(solution)/shard_map/ppermute | solution.py:22
  57.0 3.8 %collective-permute-done.3 = f32[512,128]{1,0:T(8,128)S(1)} collective-permute-done((f32[512,128]{1,0:T(8,128)S(1)}, f32[512,128]{1,0:T(8,128)S(1)}, u32[]{:S(2)}, u32[]{:S(2)}) %collective-permute-start.3) | collective-permute-done | bytes 262176 | tf_op jit(solution)/shard_map/ppermute | solution.py:27
  60.9 4.2 %fusion.110 = (f32[56,32,128]{2,1,0:T(8,128)S(1)}, f32[56,32,128]{2,1,0:T(8,128)}) fusion(f32[12,32,128]{2,1,0:T(8,128)S(1)} %bitcast.253, f32[32,32,128]{2,1,0:T(8,128)S(1)} %bitcast_subtract_fusion.1, f32[12,32,128]{2,1,0:T(8,128)S(1)} %bitcast.252, f32[64,32,128]{2,1,0:T(8,128)S(1)} %pad_maximum_fusion, f32[64,32,128]{2,1,0:T(8,128)S(1)} %pad_maximum_fusion.1, ...), kind=kLoop, calls=%fused_computation.396 | loop fusion | flops 8945664 | bytes 12977668 | tf_op jit(solution)/shard_map/add | solution.py:233
  65.2 3.2 %fusion.216 = (f32[48,32,128]{2,1,0:T(8,128)S(1)}, f32[48,32,128]{2,1,0:T(8,128)}) fusion(f32[64,32,128]{2,1,0:T(8,128)S(1)} %pad_maximum_fusion, f32[56,32,128]{2,1,0:T(8,128)S(1)} %get-tuple-element.58, f32[64,32,128]{2,1,0:T(8,128)S(1)} %pad_maximum_fusion.1, f32[]{:T(128)} %bitcast.36, pred[128]{0:T(512)(128)(4,1)S(1)} %iota_compare_fusion.13, ...), kind=kLoop, calls=%fused_computation.528 | loop fusion | flops 7274496 | bytes 11142660 | tf_op jit(solution)/shard_map/add | solution.py:233
  68.4 3.0 %fusion.324 = (f32[40,32,128]{2,1,0:T(8,128)S(1)}, f32[40,32,128]{2,1,0:T(8,128)}) fusion(f32[56,32,128]{2,1,0:T(8,128)S(1)} %get-tuple-element.58, f32[48,32,128]{2,1,0:T(8,128)S(1)} %get-tuple-element.56, f32[64,32,128]{2,1,0:T(8,128)S(1)} %pad_maximum_fusion.1, f32[]{:T(128)} %bitcast.38, pred[128]{0:T(512)(128)(4,1)S(1)} %iota_compare_fusion.13, ...), kind=kLoop, calls=%fused_computation.665 | loop fusion | flops 6062080 | bytes 9307652 | tf_op jit(solution)/shard_map/add | solution.py:233
  71.5 2.6 %select_add_fusion.1 = (f32[32,32,128]{2,1,0:T(8,128)S(1)}, f32[32,32,128]{2,1,0:T(8,128)}, f32[32,32,128]{2,1,0:T(8,128)S(1)}, f32[32,32,128]{2,1,0:T(8,128)S(1)}) fusion(f32[32,32,128]{2,1,0:T(8,128)S(1)} %bitcast.183, f32[]{:T(128)} %bitcast.41, pred[128]{0:T(512)(128)(4,1)S(1)} %iota_compare_fusion.13, pred[32]{0:T(512)(128)(4,1)S(1)} %iota_compare_fusion.14, ...), kind=kLoop, calls=%fused_computation.812 | loop fusion | flops 4849664 | bytes 8521220 | tf_op jit(solution)/shard_map/add | solution.py:233
  74.2 3.4 %collective-permute-start.4 = (f32[896,128]{1,0:T(8,128)S(1)}, f32[896,128]{1,0:T(8,128)S(1)}, u32[]{:S(2)}, u32[]{:S(2)}) collective-permute-start(f32[896,128]{1,0:T(8,128)S(1)} %pad_maximum_fusion.7), channel_id=1, source_target_pairs={{0,1},{1,2},{2,3},{3,4},{4,5},{5,6},{6,7},{7,8},{8,9},{9,10},{10,1... | collective-permute-start | bytes 1376264 | tf_op jit(solution)/shard_map/ppermute | solution.py:22
  79.4 5.8 %collective-permute-done.4 = f32[896,128]{1,0:T(8,128)S(1)} collective-permute-done((f32[896,128]{1,0:T(8,128)S(1)}, f32[896,128]{1,0:T(8,128)S(1)}, u32[]{:S(2)}, u32[]{:S(2)}) %collective-permute-start.4) | collective-permute-done | bytes 458784 | tf_op jit(solution)/shard_map/ppermute | solution.py:22
  85.3 5.9 %collective-permute-done.5 = f32[896,128]{1,0:T(8,128)S(1)} collective-permute-done((f32[896,128]{1,0:T(8,128)S(1)}, f32[896,128]{1,0:T(8,128)S(1)}, u32[]{:S(2)}, u32[]{:S(2)}) %collective-permute-start.5) | collective-permute-done | bytes 458784 | tf_op jit(solution)/shard_map/ppermute | solution.py:27
  91.3 4.0 %fusion.112 = (f32[56,32,128]{2,1,0:T(8,128)S(1)}, f32[56,32,128]{2,1,0:T(8,128)}) fusion(f32[12,32,128]{2,1,0:T(8,128)S(1)} %bitcast.255, f32[32,32,128]{2,1,0:T(8,128)S(1)} %get-tuple-element.68, f32[12,32,128]{2,1,0:T(8,128)S(1)} %bitcast.254, f32[64,32,128]{2,1,0:T(8,128)S(1)} %pad_maximum_fusion.2, f32[64,32,128]{2,1,0:T(8,128)S(1)} %pad_maximum_fusion.1, ...), kind=kLoop, calls=%fused_computation.399 | loop fusion | flops 8945664 | bytes 12977668 | tf_op jit(solution)/shard_map/add | solution.py:233
  95.4 3.3 %fusion.214 = (f32[48,32,128]{2,1,0:T(8,128)S(1)}, f32[48,32,128]{2,1,0:T(8,128)}) fusion(f32[64,32,128]{2,1,0:T(8,128)S(1)} %pad_maximum_fusion.2, f32[56,32,128]{2,1,0:T(8,128)S(1)} %get-tuple-element.50, f32[64,32,128]{2,1,0:T(8,128)S(1)} %pad_maximum_fusion.1, f32[]{:T(128)} %bitcast.53, pred[128]{0:T(512)(128)(4,1)S(1)} %iota_compare_fusion.13, ...), kind=kLoop, calls=%fused_computation.521 | loop fusion | flops 7274496 | bytes 11142660 | tf_op jit(solution)/shard_map/add | solution.py:233
  98.7 3.0 %fusion.322 = (f32[40,32,128]{2,1,0:T(8,128)S(1)}, f32[40,32,128]{2,1,0:T(8,128)}) fusion(f32[56,32,128]{2,1,0:T(8,128)S(1)} %get-tuple-element.50, f32[48,32,128]{2,1,0:T(8,128)S(1)} %get-tuple-element.48, f32[64,32,128]{2,1,0:T(8,128)S(1)} %pad_maximum_fusion.1, f32[]{:T(128)} %bitcast.55, pred[128]{0:T(512)(128)(4,1)S(1)} %iota_compare_fusion.13, ...), kind=kLoop, calls=%fused_computation.658 | loop fusion | flops 6062080 | bytes 9307652 | tf_op jit(solution)/shard_map/add | solution.py:233
  101.7 2.6 %select_add_fusion = (f32[32,32,128]{2,1,0:T(8,128)S(1)}, f32[32,32,128]{2,1,0:T(8,128)}, f32[32,32,128]{2,1,0:T(8,128)S(1)}, f32[32,32,128]{2,1,0:T(8,128)S(1)}) fusion(f32[32,32,128]{2,1,0:T(8,128)S(1)} %bitcast.184, f32[]{:T(128)} %bitcast.57, pred[128]{0:T(512)(128)(4,1)S(1)} %iota_compare_fusion.13, pred[32]{0:T(512)(128)(4,1)S(1)} %iota_compare_fusion.14, ...), kind=kLoop, calls=%fused_computation.811 | loop fusion | flops 4849664 | bytes 8521220 | tf_op jit(solution)/shard_map/add | solution.py:233
  106.1 4.9 %collective-permute-start.8 = (f32[8,128]{1,0:T(8,128)S(1)}, f32[8,128]{1,0:T(8,128)S(1)}, u32[]{:S(2)}, u32[]{:S(2)}) collective-permute-start(f32[8,128]{1,0:T(8,128)S(1)} %bitcast_subtract_fusion.2), channel_id=1, source_target_pairs={{0,1},{1,2},{2,3},{3,4},{4,5},{5,6},{6,7},{7,8},{8,9},{9,10},{10,1... | collective-permute-start | bytes 12296 | tf_op jit(solution)/shard_map/ppermute | solution.py:22
  114.3 2.3 %pad_maximum_fusion.3 = (f32[64,32,128]{2,1,0:T(8,128)}, f32[64,32,128]{2,1,0:T(8,128)S(1)}) fusion(f32[16,32,128]{2,1,0:T(8,128)S(1)} %bitcast.227, f32[32,32,128]{2,1,0:T(8,128)S(1)} %bitcast.191, f32[16,32,128]{2,1,0:T(8,128)S(1)} %bitcast.226, f32[16,32,128]{2,1,0:T(8,128)} %bitcast.209, f32[32,32,128]{2,1,0:T(8,128)S(1)} %bitcast.185, ...), kind=kLoop, calls=%fused_computation.270 | loop fusion | flops 1310720 | bytes 4194304 | tf_op jit(solution)/shard_map/concatenate | solution.py:245
  116.6 1.6 slice.1888
  118.2 1.6 slice.1889
  120.5 2.4 %fusion.3 = f32[2048,4,128]{2,0,1:T(8,128)S(1)} fusion(s32[384]{0:T(512)S(1)} %get-tuple-element.91, f32[384,4]{0,1:T(4,128)S(1)} %bitcast.260, f32[384,128]{0,1:T(8,128)S(1)} %fusion.442), kind=kOutput, calls=%fused_computation.261 | convolution fusion | flops 2416902144 | bytes 4398592 | tf_op jit(solution)/shard_map/dot_general | solution.py:103
  123.2 2.6 %slice_multiply_fusion.9 = (f32[56,32,128]{2,1,0:T(8,128)S(1)}, f32[56,32,128]{2,1,0:T(8,128)S(1)}) fusion(f32[64,32,128]{2,1,0:T(8,128)S(1)} %pad_maximum_fusion.1, f32[56,32,128]{2,1,0:T(8,128)S(1)} %bitcast.198, f32[64,32,128]{2,1,0:T(8,128)S(1)} %get-tuple-element.65, f32[12,32,128]{2,1,0:T(8,128)S(1)} %bitcast.241, f32[32,32,128]{2,1,0:T(8,128)S(1)} %copy-done.12, ...), kind=kLoop, calls=%fused_computation.535 | loop fusion | flops 8257536 | bytes 14811136 | tf_op jit(solution)/shard_map/mul | solution.py:286
  125.8 1.9 slice_multiply_fusion.15
  127.7 1.6 slice_multiply_fusion.17
  129.3 1.9 fusion.492
  132.2 4.8 %collective-permute-start.10 = (f32[896,128]{1,0:T(8,128)}, f32[896,128]{1,0:T(8,128)}, u32[]{:S(2)}, u32[]{:S(2)}) collective-permute-start(f32[896,128]{1,0:T(8,128)} %pad_maximum_fusion.11), channel_id=1, source_target_pairs={{0,1},{1,2},{2,3},{3,4},{4,5},{5,6},{6,7},{7,8},{8,9},{9,10},{10,1... | collective-permute-start | bytes 1376264 | tf_op jit(solution)/shard_map/ppermute | solution.py:22
  140.6 2.4 %fusion.1 = f32[2048,4,128]{2,0,1:T(8,128)S(1)} fusion(s32[384]{0:T(512)S(1)} %get-tuple-element.91, f32[384,4]{0,1:T(4,128)S(1)} %bitcast.259, f32[384,128]{0,1:T(8,128)S(1)} %copy-done.8), kind=kOutput, calls=%fused_computation.260 | convolution fusion | flops 2416902144 | bytes 4398592 | tf_op jit(solution)/shard_map/dot_general | solution.py:103
  144.3 3.5 %collective-permute-done.11 = f32[896,128]{1,0:T(8,128)} collective-permute-done((f32[896,128]{1,0:T(8,128)}, f32[896,128]{1,0:T(8,128)}, u32[]{:S(2)}, u32[]{:S(2)}) %collective-permute-start.11) | collective-permute-done | bytes 458784 | tf_op jit(solution)/shard_map/ppermute | solution.py:27
  150.9 2.6 %slice_multiply_fusion.8 = (f32[56,32,128]{2,1,0:T(8,128)S(1)}, f32[56,32,128]{2,1,0:T(8,128)S(1)}) fusion(f32[64,32,128]{2,1,0:T(8,128)S(1)} %pad_maximum_fusion.1, f32[56,32,128]{2,1,0:T(8,128)S(1)} %bitcast.197, f32[64,32,128]{2,1,0:T(8,128)S(1)} %get-tuple-element.63, f32[12,32,128]{2,1,0:T(8,128)S(1)} %bitcast.243, f32[32,32,128]{2,1,0:T(8,128)S(1)} %copy-done.26, ...), kind=kLoop, calls=%fused_computation.534 | loop fusion | flops 8257536 | bytes 14811136 | tf_op jit(solution)/shard_map/mul | solution.py:286
  153.5 1.9 slice_multiply_fusion.14
  158.6 2.7 %fusion.426 = (f32[32,32,128]{2,1,0:T(8,128)S(1)}, f32[32,32,128]{2,1,0:T(8,128)}) fusion(f32[56,32,128]{2,1,0:T(8,128)S(1)} %copy-done.17, f32[48,32,128]{2,1,0:T(8,128)S(1)} %copy-done.19, f32[40,32,128]{2,1,0:T(8,128)S(1)} %copy-done.21, f32[32,32,128]{2,1,0:T(8,128)S(1)} %copy-done.23, f32[56,32,128]{2,1,0:T(8,128)S(1)} %get-tuple-element.37, ...), kind=kLoop, calls=%fused_computation.774 | loop fusion | flops 6422528 | bytes 14811136 | tf_op jit(solution)/shard_map/mul | solution.py:301
  162.8 36.9 %all_to_all.10 = f32[128,2,8,128]{3,2,1,0:T(8,128)S(1)} all-to-all(f32[128,2,8,128]{3,2,1,0:T(8,128)S(1)} %copy.58), channel_id=1, replica_groups=mesh['shot'=8,'blk'=16] {'shot','blk'}, dimensions={0} | all-to-all | bytes 2097152 | tf_op jit(solution)/shard_map/all_to_all | solution.py:304
  (218 shorter events, 54.1 us)
Async XLA Ops:
  0.6 19.8 %copy-start.9 = (f32[1,32,32,128]{3,2,1,0:T(8,128)S(1)}, f32[1,32,32,128]{3,2,1,0:T(8,128)}, u32[]{:S(2)}) copy-start(f32[1,32,32,128]{3,2,1,0:T(8,128)} %param.22) | copy-start | bytes 1572868
  6.5 15.2 %copy-start.41 = (s32[1,1,128]{2,1,0:T(1,128)S(1)}, s32[1,1,128]{2,1,0:T(1,128)}, u32[]{:S(2)}) copy-start(s32[1,1,128]{2,1,0:T(1,128)} %param.20) | copy-start | bytes 1540
  7.3 20.8 %copy-start.10 = (f32[1,32,32,128]{3,2,1,0:T(8,128)S(1)}, f32[1,32,32,128]{3,2,1,0:T(8,128)}, u32[]{:S(2)}) copy-start(f32[1,32,32,128]{3,2,1,0:T(8,128)} %param.24) | copy-start | bytes 1572868
  8.6 35.6 %all-to-all-start = ((bf16[128,2,9,128]{3,1,2,0:T(2,128)(2,1)}), bf16[128,2,9,128]{3,1,2,0:T(2,128)(2,1)}, u32[]{:S(2)}, u32[]{:S(2)}) async-start(bf16[128,2,9,128]{3,1,2,0:T(2,128)(2,1)} %copy.51), calls=%async_computation | async-start | bytes 1179648 | tf_op jit(solution)/shard_map/all_to_all | solution.py:185
  21.6 17.8 %copy-start.39 = (s32[4]{0:T(128)S(1)}, s32[4]{0:T(128)}, u32[]{:S(2)}) copy-start(s32[4]{0:T(128)} %constant.229) | copy-start | bytes 52
  21.7 17.8 %copy-start.40 = (s32[4]{0:T(128)S(1)}, s32[4]{0:T(128)}, u32[]{:S(2)}) copy-start(s32[4]{0:T(128)} %constant.230) | copy-start | bytes 52
  21.7 18.4 %copy-start.29 = (f32[1,8]{1,0:T(1,128)S(1)}, f32[1,8]{1,0:T(1,128)}, u32[]{:S(2)}) copy-start(f32[1,8]{1,0:T(1,128)} %param.19) | copy-start | bytes 100
  21.7 22.4 %copy-start.37 = (s32[384]{0:T(512)S(1)}, s32[384]{0:T(512)}, u32[]{:S(2)}) copy-start(s32[384]{0:T(512)} %constant.176.clone.1) | copy-start | bytes 4612
  22.7 19.7 %collective-permute-start = (f32[897,128]{1,0:T(8,128)}, f32[897,128]{1,0:T(8,128)}, u32[]{:S(2)}, u32[]{:S(2)}) collective-permute-start(f32[897,128]{1,0:T(8,128)} %get-tuple-element.104), channel_id=1, source_target_pairs={{0,1},{1,2},{2,3},{3,4},{4,5},{5,6},{6,7},{7,8},{8,9},{9,10},{10,1... | collective-permute-start | bytes 1377800 | tf_op jit(solution)/shard_map/ppermute | solution.py:22
  26.8 14.0 %collective-permute-start.1 = (f32[897,128]{1,0:T(8,128)}, f32[897,128]{1,0:T(8,128)}, u32[]{:S(2)}, u32[]{:S(2)}) collective-permute-start(f32[897,128]{1,0:T(8,128)} %get-tuple-element.105), channel_id=1, source_target_pairs={{1,0},{2,1},{3,2},{4,3},{5,4},{6,5},{7,6},{8,7},{9,8},{10,9},{11,1... | collective-permute-start | bytes 1377800 | tf_op jit(solution)/shard_map/ppermute | solution.py:27
  29.3 14.9 %copy-start.11 = (f32[32,32,128]{2,1,0:T(8,128)}, f32[32,32,128]{2,1,0:T(8,128)S(1)}, u32[]{:S(2)}) copy-start(f32[32,32,128]{2,1,0:T(8,128)S(1)} %bitcast_subtract_fusion) | copy-start | bytes 1572868
  30.2 75.9 %collective-permute-start.6 = (f32[896,128]{1,0:T(8,128)}, f32[896,128]{1,0:T(8,128)}, u32[]{:S(2)}, u32[]{:S(2)}) collective-permute-start(f32[896,128]{1,0:T(8,128)} %pad_maximum_fusion.9), channel_id=1, source_target_pairs={{0,1},{1,2},{2,3},{3,4},{4,5},{5,6},{6,7},{7,8},{8,9},{9,10},{10,1... | collective-permute-start | bytes 1376264 | tf_op jit(solution)/shard_map/ppermute | solution.py:22
  35.7 70.4 %collective-permute-start.7 = (f32[896,128]{1,0:T(8,128)}, f32[896,128]{1,0:T(8,128)}, u32[]{:S(2)}, u32[]{:S(2)}) collective-permute-start(f32[896,128]{1,0:T(8,128)} %pad_maximum_fusion.10), channel_id=1, source_target_pairs={{1,0},{2,1},{3,2},{4,3},{5,4},{6,5},{7,6},{8,7},{9,8},{10,9},{11,1... | collective-permute-start | bytes 1376264 | tf_op jit(solution)/shard_map/ppermute | solution.py:27
  39.3 8.9 %copy-start.34 = (s32[128]{0:T(128)}, s32[128]{0:T(128)S(1)}, u32[]{:S(2)}) copy-start(s32[128]{0:T(128)S(1)} %multiply_add_fusion.1) | copy-start | bytes 1540
  44.2 76.2 %copy-start.7 = (f32[384,128]{0,1:T(8,128)}, f32[384,128]{0,1:T(8,128)S(1)}, u32[]{:S(2)}) copy-start(f32[384,128]{0,1:T(8,128)S(1)} %fusion.442) | copy-start | bytes 589828
  48.9 8.1 %collective-permute-start.2 = (f32[512,128]{1,0:T(8,128)S(1)}, f32[512,128]{1,0:T(8,128)S(1)}, u32[]{:S(2)}, u32[]{:S(2)}) collective-permute-start(f32[512,128]{1,0:T(8,128)S(1)} %bitcast.258), channel_id=1, source_target_pairs={{0,1},{1,2},{2,3},{3,4},{4,5},{5,6},{6,7},{7,8},{8,9},{9,10},{10,1... | collective-permute-start | bytes 786440 | tf_op jit(solution)/shard_map/ppermute | solution.py:22
  52.9 8.0 %collective-permute-start.3 = (f32[512,128]{1,0:T(8,128)S(1)}, f32[512,128]{1,0:T(8,128)S(1)}, u32[]{:S(2)}, u32[]{:S(2)}) collective-permute-start(f32[512,128]{1,0:T(8,128)S(1)} %bitcast.257), channel_id=1, source_target_pairs={{1,0},{2,1},{3,2},{4,3},{5,4},{6,5},{7,6},{8,7},{9,8},{10,9},{11,1... | collective-permute-start | bytes 786440 | tf_op jit(solution)/shard_map/ppermute | solution.py:27
  57.0 11.4 %copy-start.13 = (f32[512,128]{1,0:T(8,128)}, f32[512,128]{1,0:T(8,128)S(1)}, u32[]{:S(2)}) copy-start(f32[512,128]{1,0:T(8,128)S(1)} %collective-permute-done.2) | copy-start | bytes 786436
  60.8 7.6 %copy-start.15 = (f32[512,128]{1,0:T(8,128)}, f32[512,128]{1,0:T(8,128)S(1)}, u32[]{:S(2)}) copy-start(f32[512,128]{1,0:T(8,128)S(1)} %collective-permute-done.3) | copy-start | bytes 786436
  74.2 11.1 %collective-permute-start.4 = (f32[896,128]{1,0:T(8,128)S(1)}, f32[896,128]{1,0:T(8,128)S(1)}, u32[]{:S(2)}, u32[]{:S(2)}) collective-permute-start(f32[896,128]{1,0:T(8,128)S(1)} %pad_maximum_fusion.7), channel_id=1, source_target_pairs={{0,1},{1,2},{2,3},{3,4},{4,5},{5,6},{6,7},{7,8},{8,9},{9,10},{10,1... | collective-permute-start | bytes 1376264 | tf_op jit(solution)/shard_map/ppermute | solution.py:22
  77.7 13.5 %collective-permute-start.5 = (f32[896,128]{1,0:T(8,128)S(1)}, f32[896,128]{1,0:T(8,128)S(1)}, u32[]{:S(2)}, u32[]{:S(2)}) collective-permute-start(f32[896,128]{1,0:T(8,128)S(1)} %pad_maximum_fusion.8), channel_id=1, source_target_pairs={{1,0},{2,1},{3,2},{4,3},{5,4},{6,5},{7,6},{8,7},{9,8},{10,9},{11,1... | collective-permute-start | bytes 1376264 | tf_op jit(solution)/shard_map/ppermute | solution.py:27
  106.1 13.7 %collective-permute-start.8 = (f32[8,128]{1,0:T(8,128)S(1)}, f32[8,128]{1,0:T(8,128)S(1)}, u32[]{:S(2)}, u32[]{:S(2)}) collective-permute-start(f32[8,128]{1,0:T(8,128)S(1)} %bitcast_subtract_fusion.2), channel_id=1, source_target_pairs={{0,1},{1,2},{2,3},{3,4},{4,5},{5,6},{6,7},{7,8},{8,9},{9,10},{10,1... | collective-permute-start | bytes 12296 | tf_op jit(solution)/shard_map/ppermute | solution.py:22
  111.0 8.8 %collective-permute-start.9 = (f32[8,128]{1,0:T(8,128)S(1)}, f32[8,128]{1,0:T(8,128)S(1)}, u32[]{:S(2)}, u32[]{:S(2)}) collective-permute-start(f32[8,128]{1,0:T(8,128)S(1)} %bitcast_subtract_fusion.2), channel_id=1, source_target_pairs={{1,0},{2,1},{3,2},{4,3},{5,4},{6,5},{7,6},{8,7},{9,8},{10,9},{11,1... | collective-permute-start | bytes 12296 | tf_op jit(solution)/shard_map/ppermute | solution.py:27
  129.3 11.2 %copy-start.8 = (f32[384,128]{0,1:T(8,128)S(1)}, f32[384,128]{0,1:T(8,128)}, u32[]{:S(2)}) copy-start(f32[384,128]{0,1:T(8,128)} %copy-done.7) | copy-start | bytes 589828
  131.3 17.4 %copy-start = (f32[32,32,128]{2,1,0:T(8,128)}, f32[32,32,128]{2,1,0:T(8,128)S(1)}, u32[]{:S(2)}) copy-start(f32[32,32,128]{2,1,0:T(8,128)S(1)} %get-tuple-element.70) | copy-start | bytes 1572868
  132.2 11.0 %collective-permute-start.10 = (f32[896,128]{1,0:T(8,128)}, f32[896,128]{1,0:T(8,128)}, u32[]{:S(2)}, u32[]{:S(2)}) collective-permute-start(f32[896,128]{1,0:T(8,128)} %pad_maximum_fusion.11), channel_id=1, source_target_pairs={{0,1},{1,2},{2,3},{3,4},{4,5},{5,6},{6,7},{7,8},{8,9},{9,10},{10,1... | collective-permute-start | bytes 1376264 | tf_op jit(solution)/shard_map/ppermute | solution.py:22
  137.8 9.9 %collective-permute-start.11 = (f32[896,128]{1,0:T(8,128)}, f32[896,128]{1,0:T(8,128)}, u32[]{:S(2)}, u32[]{:S(2)}) collective-permute-start(f32[896,128]{1,0:T(8,128)} %pad_maximum_fusion.12), channel_id=1, source_target_pairs={{1,0},{2,1},{3,2},{4,3},{5,4},{6,5},{7,6},{8,7},{9,8},{10,9},{11,1... | collective-permute-start | bytes 1376264 | tf_op jit(solution)/shard_map/ppermute | solution.py:27
  143.0 5.7 %copy-start.14 = (f32[512,128]{1,0:T(8,128)S(1)}, f32[512,128]{1,0:T(8,128)}, u32[]{:S(2)}) copy-start(f32[512,128]{1,0:T(8,128)} %copy-done.13) | copy-start | bytes 786436
  143.0 5.7 %copy-start.16 = (f32[512,128]{1,0:T(8,128)S(1)}, f32[512,128]{1,0:T(8,128)}, u32[]{:S(2)}) copy-start(f32[512,128]{1,0:T(8,128)} %copy-done.15) | copy-start | bytes 786436
  143.2 7.7 %copy-start.26 = (f32[32,32,128]{2,1,0:T(8,128)S(1)}, f32[32,32,128]{2,1,0:T(8,128)}, u32[]{:S(2)}) copy-start(f32[32,32,128]{2,1,0:T(8,128)} %get-tuple-element.69) | copy-start | bytes 1572868
  162.2 38.1 %copy-start.31 = (s32[256]{0:T(256)S(1)}, s32[256]{0:T(256)}, u32[]{:S(2)}) copy-start(s32[256]{0:T(256)} %copy-done.30) | copy-start | bytes 3076
  162.2 38.1 %copy-start.33 = (pred[256]{0:T(512)(128)(4,1)S(1)}, pred[256]{0:T(512)(128)(4,1)}, u32[]{:S(2)}) copy-start(pred[256]{0:T(512)(128)(4,1)} %copy-done.32) | copy-start | bytes 772
  (23 other events, 52.7 us)
